TPU v7x, 32 devices: a whole 2x2x4 slice. The times are simulated.
32 devices in a mesh: ev: 8 (over z, y), col: 4 (over x, core).
Axes of the slice: x: 2, y: 2, z: 4, core: 2. Of those that a mesh axis runs over, the one named last changes fastest.
Arguments:
- panel: bfloat16 [256, 131072], P('col', 'ev'), may hold values from -12 to 12
- signs: int32 [131072], P('ev'), may hold values from -1 to 1, as said below
- offsets: int32 [2048], replicated, may hold values from 0 to 63
Outputs:
- gram: float32 [256, 256], P('col')
Inputs may be any that keep to these rules, and one draw needn't show every extreme that they name: `signs`: every entry is -1 or +1.
All inputs are finite; a program needn't handle non-finite values.
Results may differ from a plain program's by a relative error of at most 0.0003.
Values sent between devices are 32-bit elements; how exact they have to be, the bound alone decides.
No kernel may reach another device: no remote copies, remote signals or barrier semaphores. Data moves between devices by JAX's collectives and lax.ppermute only.
A program may use at most 64 MiB of HBM per device.

v0:
```python
import math
import jax
import jax.numpy as jnp
from jax import lax
from jax.sharding import PartitionSpec as P

STRIDE = 64


def swapped(value, axis, stride):
    mask = 2**stride
    pairs = [(source, source ^ mask) for source in range(lax.axis_size(axis))]
    return lax.ppermute(value, axis, pairs)


def hadamard(order):
    index = jnp.arange(order, dtype=jnp.int32)
    both = index[:, None] & index[None, :]
    parity = jnp.zeros((order, order), jnp.int32)
    for level in range(order.bit_length() - 1):
        parity = parity + (both >> level & 1)
    return (1 - 2 * (parity % 2)).astype(jnp.float32)


def pick_local(values, offsets, my_index, strata):
    columns = values.shape[0]
    chosen = lax.dynamic_slice_in_dim(offsets, my_index * strata, strata)
    grouped = values.reshape(columns, strata, STRIDE)
    return jnp.take_along_axis(grouped, chosen[None, :, None], axis=2)[:, :, 0]


def per_device(panel, signs, offsets):
    columns, length = panel.shape
    groups = lax.axis_size("ev")
    my_index = lax.axis_index("ev")
    inner_len = length // 128
    strata = length // STRIDE
    high = lax.Precision.HIGHEST
    signed = panel * signs.astype(jnp.bfloat16)[None, :]
    blocks = signed.reshape(columns, 128, inner_len)
    first = jnp.einsum(
        "xa,cab->cxb",
        hadamard(128).astype(jnp.bfloat16),
        blocks,
        preferred_element_type=jnp.float32,
    )
    local = jnp.einsum("yb,cxb->cxy", hadamard(inner_len), first, precision=high).reshape(
        columns, length
    )
    total_events = length * groups
    scale = 1.0 / math.sqrt(total_events * (total_events // STRIDE))
    values = local
    for level in range(groups.bit_length() - 1):
        partner = swapped(values, "ev", level)
        upper_half = my_index >> level & 1 == 1
        values = jnp.where(upper_half, partner - values, values + partner)
    picked = pick_local(values, offsets, my_index, strata)
    sketch = picked * scale
    partial_gram = jnp.dot(
        sketch,
        lax.all_gather(sketch, "col", axis=0, tiled=True).T,
        precision=high,
        preferred_element_type=jnp.float32,
    )
    return lax.psum(partial_gram, "ev")


def solution(mesh):
    return jax.shard_map(
        per_device,
        mesh=mesh,
        in_specs=(P("col", "ev"), P("ev"), P()),
        out_specs=P("col", None),
        check_vma=False,
    )
```

profile of v0, /device:TPU:0, one launch (start us, length us, event | category | flops | bytes accessed | tf_op | source)
XLA Modules:
  0.0 503.6 jit_solution(14643924601332694307)
XLA Ops:
  6.5 0.8 convert_element_type.12
  7.4 1.9 multiply_bitcast_fusion
  9.2 0.6 copy.12
  9.8 0.8 fusion.12
  10.6 6.7 %fusion = f32[64,128,128]{2,1,0:T(8,128)S(1)} fusion(f32[64,128,128]{2,1,0:T(8,128)S(1)} %fusion.12), kind=kOutput, calls=%fused_computation.2 | convolution fusion | flops 1611186176 | bytes 8388608 | tf_op jit(solution)/shard_map/yb,cxb->cxy/dot_general | solution.py:47
  17.3 4.3 copy.17
  21.6 3.0 collective-permute-start
  24.6 90.9 %collective-permute-done = f32[64,16384]{1,0:T(8,128)} collective-permute-done((f32[64,16384]{1,0:T(8,128)}, f32[64,16384]{1,0:T(8,128)}, u32[]{:S(2)}, u32[]{:S(2)}) %collective-permute-start) | collective-permute-done | bytes 4194336 | tf_op jit(solution)/shard_map/ppermute | solution.py:13
  115.5 8.4 %add_select_fusion.2 = f32[64,16384]{1,0:T(8,128)} fusion(f32[64,16384]{1,0:T(8,128)} %collective-permute-done, pred[]{:T(512)S(6)} %eq.14, f32[8,8,128,128]{3,2,1,0:T(8,128)} %bitcast.28), kind=kLoop, calls=%fused_computation.6 | loop fusion | flops 3145728 | bytes 12582913 | tf_op jit(solution)/shard_map/jit(_where)/select_n | solution.py:56
  123.9 1.8 collective-permute-start.1
  125.7 90.3 %collective-permute-done.1 = f32[64,16384]{1,0:T(8,128)} collective-permute-done((f32[64,16384]{1,0:T(8,128)}, f32[64,16384]{1,0:T(8,128)}, u32[]{:S(2)}, u32[]{:S(2)}) %collective-permute-start.1) | collective-permute-done | bytes 4194336 | tf_op jit(solution)/shard_map/ppermute | solution.py:13
  216.0 5.9 %add_select_fusion.1 = f32[64,16384]{1,0:T(8,128)} fusion(f32[64,16384]{1,0:T(8,128)} %add_select_fusion.2, f32[64,16384]{1,0:T(8,128)} %collective-permute-done.1, pred[]{:T(512)S(6)} %eq.13), kind=kLoop, calls=%fused_computation.5 | loop fusion | flops 3145728 | bytes 12582913 | tf_op jit(solution)/shard_map/jit(_where)/select_n | solution.py:56
  221.8 2.5 collective-permute-start.2
  224.3 0.8 compare_and_fusion
  225.1 178.6 %collective-permute-done.2 = f32[64,16384]{1,0:T(8,128)} collective-permute-done((f32[64,16384]{1,0:T(8,128)}, f32[64,16384]{1,0:T(8,128)}, u32[]{:S(2)}, u32[]{:S(2)}) %collective-permute-start.2) | collective-permute-done | bytes 4194336 | tf_op jit(solution)/shard_map/ppermute | solution.py:13
  403.8 5.9 %add_select_fusion = f32[64,16384]{1,0:T(8,128)} fusion(f32[64,16384]{1,0:T(8,128)} %add_select_fusion.1, f32[64,16384]{1,0:T(8,128)} %collective-permute-done.2, pred[]{:T(512)S(6)} %eq.12), kind=kLoop, calls=%fused_computation.4 | loop fusion | flops 3145728 | bytes 12582913 | tf_op jit(solution)/shard_map/jit(_where)/select_n | solution.py:56
  409.6 6.9 %copy.8 = f32[64,16384]{0,1:T(8,128)} copy(f32[64,16384]{1,0:T(8,128)} %add_select_fusion) | data formatting | bytes 8388608 | tf_op jit(solution)/shard_map/jit(_where)/select_n | solution.py:56
  416.5 2.3 gather_fusion
  418.9 0.1 fusion.3
  419.0 0.1 copy.9
  419.1 5.8 %all_gather.3 = f32[256,256]{1,0:T(8,128)S(1)} all-gather(f32[64,256]{1,0:T(8,128)S(1)} %copy.9), channel_id=1, replica_groups=mesh['ev'=8,'col'=4] {'col'}, dimensions={0}, use_global_device_ids=true | all-gather | bytes 327680 | tf_op jit(solution)/shard_map/all_gather | solution.py:61
  424.8 1.1 fusion.2
  425.9 69.4 %all-reduce.2.cloned.1.call-done = f32[64,256]{1,0:T(8,128)} async-done(((f32[64,256]{1,0:T(8,128)}), f32[64,256]{1,0:T(8,128)}) %all-reduce.2.cloned.1.call-update) | async-done | bytes 65552 | tf_op jit(solution)/shard_map/psum | solution.py:65
  495.3 1.5 copy.19
  (7 shorter events, 0.0 us)
Async XLA Ops:
  6.5 488.8 %all-reduce.2.cloned.1.call-start = ((), (), s32[]{:S(2)}) async-start(), calls=%async_computation | async-start | bytes 131072 | tf_op jit(solution)/shard_map/psum | solution.py:65
  17.3 4.3 copy-start
  21.6 93.9 %collective-permute-start = (f32[64,16384]{1,0:T(8,128)}, f32[64,16384]{1,0:T(8,128)}, u32[]{:S(2)}, u32[]{:S(2)}) collective-permute-start(f32[64,16384]{1,0:T(8,128)} %bitcast.26), channel_id=1, source_target_pairs={{0,4},{4,0},{8,12},{12,8},{16,20},{20,16},{24,28},{28,24},{1,5},{5... | collective-permute-start | bytes 12582920 | tf_op jit(solution)/shard_map/ppermute | solution.py:13
  123.9 92.1 %collective-permute-start.1 = (f32[64,16384]{1,0:T(8,128)}, f32[64,16384]{1,0:T(8,128)}, u32[]{:S(2)}, u32[]{:S(2)}) collective-permute-start(f32[64,16384]{1,0:T(8,128)} %add_select_fusion.2), channel_id=1, source_target_pairs={{0,8},{4,12},{8,0},{12,4},{16,24},{20,28},{24,16},{28,20},{1,9},{5... | collective-permute-start | bytes 12582920 | tf_op jit(solution)/shard_map/ppermute | solution.py:13
  221.8 181.9 %collective-permute-start.2 = (f32[64,16384]{1,0:T(8,128)}, f32[64,16384]{1,0:T(8,128)}, u32[]{:S(2)}, u32[]{:S(2)}) collective-permute-start(f32[64,16384]{1,0:T(8,128)} %add_select_fusion.1), channel_id=1, source_target_pairs={{0,16},{4,20},{8,24},{12,28},{16,0},{20,4},{24,8},{28,12},{1,17},{... | collective-permute-start | bytes 12582920 | tf_op jit(solution)/shard_map/ppermute | solution.py:13
Sparse Core Ops, SparseCore 0:
  426.1 69.1 all-reduce.1
where the time goes:
time: 504 us
  waiting for transfers between devices  429 us (85%)
  other arithmetic  23.7 us (5%)
  local copies, waits for them, and re-layouts  15.7 us (3%)
  between operations  13.4 us (3%)
  matrix products  8.53 us (2%)
  starting transfers between devices  7.27 us (1%)
  blocking collectives  5.79 us (1%)
    ppermute x3, waiting for transfers between devices, swapped(): return lax.ppermute(value, axis, pairs)  360 us
    psum x1, waiting for transfers between devices, per_device(): return lax.psum(partial_gram, 'ev')  69.4 us
    select_n x3, other arithmetic, per_device(): values = jnp.where(upper_half, partner - values, values + partner)  20.1 us
  transfers between devices with their start and end apart: 4, of which 4 were waited for; matrix products, arithmetic and copies ran while one was open for 0% of the time, Pallas kernels for 0%

commit v1 on v0

--- a/solution.py
+++ b/solution.py
@@ -62,7 +62,7 @@
         precision=high,
         preferred_element_type=jnp.float32,
     )
-    return lax.psum(partial_gram, "ev")
+    return jnp.sum(lax.all_gather(partial_gram, "ev"), axis=0)
 
 
 def solution(mesh):

time: 504 us -> 451 us (0.89)
  waiting for transfers between devices: 429 us -> 360 us
  blocking collectives: 5.79 us -> 37.2 us
  between operations: 13.4 us -> 0.07 us
    psum x1 -> x0, waiting for transfers between devices: 69.4 us -> none  [per_device(): return lax.psum(partial_gram, 'ev')]
    all_gather x0 -> x1, blocking collectives: none -> 31.4 us  [per_device(): return jnp.sum(lax.all_gather(partial_gram, 'ev'), axis=0)]
  transfers between devices with their start and end apart: 4 -> 3, of which waited for: 4 -> 3; matrix products, arithmetic and copies ran while one was open for 0% -> 0% of each run, Pallas kernels for 0% -> 0%
where the time goes in v1:
time: 451 us
  waiting for transfers between devices  360 us (80%)
  blocking collectives  37.2 us (8%)
  other arithmetic  24.4 us (5%)
  local copies, waits for them, and re-layouts  14.2 us (3%)
  matrix products  8.1 us (2%)
  starting transfers between devices  7.26 us (2%)
    ppermute x3, waiting for transfers between devices, swapped(): return lax.ppermute(value, axis, pairs)  360 us
    all_gather x1, blocking collectives, per_device(): return jnp.sum(lax.all_gather(partial_gram, 'ev'), axis=0)  31.4 us
    select_n x3, other arithmetic, per_device(): values = jnp.where(upper_half, partner - values, values + partner)  20.1 us
  transfers between devices with their start and end apart: 3, of which 3 were waited for; matrix products, arithmetic and copies ran while one was open for 0% of the time, Pallas kernels for 0%

profile of v1, /device:TPU:0, one launch (start us, length us, event | category | flops | bytes accessed | tf_op | source)
XLA Modules:
  0.0 451.0 jit_solution(9383943741397265987)
XLA Ops:
  0.0 0.8 convert_element_type.12
  0.8 1.9 multiply_bitcast_fusion
  2.7 0.6 copy.12
  3.3 0.8 fusion.12
  4.1 6.9 %fusion = f32[64,128,128]{2,1,0:T(8,128)S(1)} fusion(f32[64,128,128]{2,1,0:T(8,128)S(1)} %fusion.12), kind=kOutput, calls=%fused_computation.2 | convolution fusion | flops 1611186176 | bytes 8388608 | tf_op jit(solution)/shard_map/yb,cxb->cxy/dot_general | solution.py:47
  11.0 4.3 copy.17
  15.3 3.0 collective-permute-start
  18.3 90.9 %collective-permute-done = f32[64,16384]{1,0:T(8,128)} collective-permute-done((f32[64,16384]{1,0:T(8,128)}, f32[64,16384]{1,0:T(8,128)}, u32[]{:S(2)}, u32[]{:S(2)}) %collective-permute-start) | collective-permute-done | bytes 4194336 | tf_op jit(solution)/shard_map/ppermute | solution.py:13
  109.1 8.4 %add_select_fusion.2 = f32[64,16384]{1,0:T(8,128)} fusion(f32[64,16384]{1,0:T(8,128)} %collective-permute-done, pred[]{:T(512)S(6)} %eq.14, f32[8,8,128,128]{3,2,1,0:T(8,128)} %bitcast.29), kind=kLoop, calls=%fused_computation.6 | loop fusion | flops 3145728 | bytes 12582913 | tf_op jit(solution)/shard_map/jit(_where)/select_n | solution.py:56
  117.5 1.8 collective-permute-start.1
  119.3 90.3 %collective-permute-done.1 = f32[64,16384]{1,0:T(8,128)} collective-permute-done((f32[64,16384]{1,0:T(8,128)}, f32[64,16384]{1,0:T(8,128)}, u32[]{:S(2)}, u32[]{:S(2)}) %collective-permute-start.1) | collective-permute-done | bytes 4194336 | tf_op jit(solution)/shard_map/ppermute | solution.py:13
  209.6 5.9 %add_select_fusion.1 = f32[64,16384]{1,0:T(8,128)} fusion(f32[64,16384]{1,0:T(8,128)} %add_select_fusion.2, f32[64,16384]{1,0:T(8,128)} %collective-permute-done.1, pred[]{:T(512)S(6)} %eq.13), kind=kLoop, calls=%fused_computation.5 | loop fusion | flops 3145728 | bytes 12582913 | tf_op jit(solution)/shard_map/jit(_where)/select_n | solution.py:56
  215.5 2.5 collective-permute-start.2
  218.0 0.8 compare_and_fusion
  218.8 178.7 %collective-permute-done.2 = f32[64,16384]{1,0:T(8,128)} collective-permute-done((f32[64,16384]{1,0:T(8,128)}, f32[64,16384]{1,0:T(8,128)}, u32[]{:S(2)}, u32[]{:S(2)}) %collective-permute-start.2) | collective-permute-done | bytes 4194336 | tf_op jit(solution)/shard_map/ppermute | solution.py:13
  397.4 5.9 %add_select_fusion = f32[64,16384]{1,0:T(8,128)} fusion(f32[64,16384]{1,0:T(8,128)} %add_select_fusion.1, f32[64,16384]{1,0:T(8,128)} %collective-permute-done.2, pred[]{:T(512)S(6)} %eq.12), kind=kLoop, calls=%fused_computation.4 | loop fusion | flops 3145728 | bytes 12582913 | tf_op jit(solution)/shard_map/jit(_where)/select_n | solution.py:56
  403.3 6.9 %copy.8 = f32[64,16384]{0,1:T(8,128)} copy(f32[64,16384]{1,0:T(8,128)} %add_select_fusion) | data formatting | bytes 8388608 | tf_op jit(solution)/shard_map/jit(_where)/select_n | solution.py:56
  410.2 2.3 gather_fusion
  412.5 0.1 fusion.3
  412.6 0.1 copy.9
  412.7 5.8 %all_gather.9 = f32[256,256]{1,0:T(8,128)S(1)} all-gather(f32[64,256]{1,0:T(8,128)S(1)} %copy.9), channel_id=1, replica_groups=mesh['ev'=8,'col'=4] {'col'}, dimensions={0}, use_global_device_ids=true | all-gather | bytes 327680 | tf_op jit(solution)/shard_map/all_gather | solution.py:61
  418.5 0.4 fusion.2
  419.0 31.4 %all-gather = f32[512,256]{1,0:T(8,128)S(1)} all-gather(f32[64,256]{1,0:T(8,128)S(1)} %fusion.2), channel_id=2, replica_groups=mesh['ev'=8,'col'=4] {'ev'}, dimensions={0}, use_global_device_ids=true | all-gather | bytes 589824 | tf_op jit(solution)/shard_map/all_gather | solution.py:65
  450.3 0.7 reduce_sum.9
  (5 shorter events, 0.0 us)
Async XLA Ops:
  10.9 4.3 copy-start
  15.3 93.9 %collective-permute-start = (f32[64,16384]{1,0:T(8,128)}, f32[64,16384]{1,0:T(8,128)}, u32[]{:S(2)}, u32[]{:S(2)}) collective-permute-start(f32[64,16384]{1,0:T(8,128)} %bitcast.27), channel_id=1, source_target_pairs={{0,4},{4,0},{8,12},{12,8},{16,20},{20,16},{24,28},{28,24},{1,5},{5... | collective-permute-start | bytes 12582920 | tf_op jit(solution)/shard_map/ppermute | solution.py:13
  117.5 92.1 %collective-permute-start.1 = (f32[64,16384]{1,0:T(8,128)}, f32[64,16384]{1,0:T(8,128)}, u32[]{:S(2)}, u32[]{:S(2)}) collective-permute-start(f32[64,16384]{1,0:T(8,128)} %add_select_fusion.2), channel_id=1, source_target_pairs={{0,8},{4,12},{8,0},{12,4},{16,24},{20,28},{24,16},{28,20},{1,9},{5... | collective-permute-start | bytes 12582920 | tf_op jit(solution)/shard_map/ppermute | solution.py:13
  215.5 181.9 %collective-permute-start.2 = (f32[64,16384]{1,0:T(8,128)}, f32[64,16384]{1,0:T(8,128)}, u32[]{:S(2)}, u32[]{:S(2)}) collective-permute-start(f32[64,16384]{1,0:T(8,128)} %add_select_fusion.1), channel_id=1, source_target_pairs={{0,16},{4,20},{8,24},{12,28},{16,0},{20,4},{24,8},{28,12},{1,17},{... | collective-permute-start | bytes 12582920 | tf_op jit(solution)/shard_map/ppermute | solution.py:13
